TPU v7x, 32 devices: a whole 2x2x4 slice. The times are simulated.
32 devices in a mesh: dp: 2 (over x), expert: 4 (over y, core), tensor: 4 (over z).
Axes of the slice: x: 2, y: 2, z: 4, core: 2. Of those that a mesh axis runs over, the one named last changes fastest.
Arguments:
- output_grad: bfloat16 [2048, 4096], P(('dp', 'expert'), 'tensor'), may hold values from -6 to 6
- expert_ids: int32 [2048, 2], P(('dp', 'expert')), may hold values from 0 to 3, all different within a row; in each aligned block of 256 rows (0 to 255, 256 to 511, ...) at most 192 rows name the same one
- router_weights: bfloat16 [2048, 2], P(('dp', 'expert')), may hold values from 0.099609375 to 0.8984375
- gate_preact: bfloat16 [4, 1536, 14336], P('expert', 'dp', 'tensor'), may hold values from -6 to 6
- up_preact: bfloat16 [4, 1536, 14336], P('expert', 'dp', 'tensor'), may hold values from -6 to 6
- down_weight: bfloat16 [4, 14336, 4096], P('expert', 'tensor', 'dp'), may hold values from -0.046875 to 0.046875
Outputs:
- gate_preact_grad: bfloat16 [4, 1536, 14336], P('expert', 'dp', 'tensor')
- up_preact_grad: bfloat16 [4, 1536, 14336], P('expert', 'dp', 'tensor')
- down_grad: bfloat16 [4, 14336, 4096], P('expert', 'tensor', 'dp')
- router_grad: float32 [2048, 2], P(('dp', 'expert'))
Inputs may be any that keep to these rules, and one draw needn't show every extreme that they name: `expert_ids`: the ids of one token differ. Among the 256 rows of one device no expert is named by more than 192 rows, and in every draw some expert is named by exactly 192 rows of some device.
All inputs are finite; a program needn't handle non-finite values.
Results may differ from a plain program's by a relative error of at most 0.007.
Values may be sent and summed in bfloat16 or wider, within the bound.
No kernel may reach another device: no remote copies, remote signals or barrier semaphores. Data moves between devices by JAX's collectives and lax.ppermute only.
A program may use at most 192 MiB of HBM per device.

v0:
```python
import jax
import jax.numpy as jnp
from jax import lax
from jax.sharding import PartitionSpec as P

PARTIAL_DTYPE = jnp.float32


def silu_parts(values):
    sigma = jax.nn.sigmoid(values)
    return (values * sigma, sigma * (1.0 + values * (1.0 - sigma)))


def swap_dp(value):
    return lax.ppermute(value, "dp", perm=[(0, 1), (1, 0)])


def local(output_grad, expert_ids, router_weights, gate_preact, up_preact, down_weight):
    expert_count = lax.axis_size("expert")
    tensor_count = lax.axis_size("tensor")
    replica = lax.axis_index("dp")
    part = lax.axis_index("tensor")
    tokens_here = expert_ids.shape[0]
    choices_each = expert_ids.shape[1]
    capacity = gate_preact.shape[1] // expert_count
    flat_ids = expert_ids.reshape(-1)
    one_hot = (flat_ids[:, None] == jnp.arange(expert_count, dtype=jnp.int32)).astype(jnp.int32)
    earlier = jnp.cumsum(one_hot, axis=0) - one_hot
    slot_index = jnp.sum(earlier * one_hot, axis=1)
    target = (flat_ids * capacity + slot_index).reshape(tokens_here, choices_each)
    columns = jnp.arange(expert_count * capacity, dtype=jnp.int32)
    matches = [target[:, which][:, None] == columns[None, :] for which in range(choices_each)]
    selector = jnp.zeros((tokens_here, expert_count * capacity), jnp.bfloat16)
    gate_table = jnp.zeros((tokens_here, expert_count * capacity), jnp.float32)
    for which in range(choices_each):
        selector = jnp.where(matches[which], jnp.bfloat16(1.0), selector)
        gate_table = jnp.where(
            matches[which], router_weights[:, which : which + 1].astype(jnp.float32), gate_table
        )
    gate_send = jnp.sum(gate_table, axis=0).astype(jnp.bfloat16).reshape(expert_count, capacity)
    gate_float = gate_preact[0].astype(jnp.float32)
    up_float = up_preact[0].astype(jnp.float32)
    active, slope = silu_parts(gate_float)
    hidden = (active * up_float).astype(jnp.bfloat16)
    contract_rows = (((0,), (0,)), ((), ()))
    contract_cols = (((1,), (1,)), ((), ()))
    outgoing = lax.dot_general(
        selector, output_grad, contract_rows, preferred_element_type=jnp.float32
    )
    outgoing = outgoing.astype(jnp.bfloat16).reshape(expert_count, capacity, -1)
    hidden, outgoing = lax.optimization_barrier((hidden, outgoing))
    hidden_other = swap_dp(hidden)
    received = lax.all_to_all(outgoing, "expert", split_axis=0, concat_axis=0, tiled=True)
    gate_slots = lax.all_to_all(gate_send, "expert", split_axis=0, concat_axis=0, tiled=True)
    slots = expert_count * capacity
    narrow_rows = received.reshape(slots, -1)
    gate_bf16 = gate_slots.reshape(-1)
    gate_column = gate_bf16.astype(jnp.float32)[:, None]
    fragment = lax.all_gather(narrow_rows, "tensor", axis=1, tiled=True)
    width = fragment.shape[1]
    half = width // 2
    piece = half // tensor_count
    own_rows = lax.dynamic_slice_in_dim(fragment, replica * half, half, axis=1)
    send_rows = lax.dynamic_slice_in_dim(
        fragment, (1 - replica) * half + part * piece, piece, axis=1
    )
    other_piece = swap_dp(send_rows)
    other_rows = lax.all_gather(other_piece, "tensor", axis=1, tiled=True)
    hidden_other, other_rows = lax.optimization_barrier((hidden_other, other_rows))
    other_gates = swap_dp(gate_bf16).astype(jnp.float32)[:, None]
    local_weight = down_weight[0]
    partial_other = lax.dot_general(
        other_rows, local_weight, contract_cols, preferred_element_type=jnp.float32
    )
    partial_back = swap_dp(partial_other.astype(PARTIAL_DTYPE)).astype(jnp.float32)
    partial_own = lax.dot_general(
        own_rows, local_weight, contract_cols, preferred_element_type=jnp.float32
    )
    scaled_own = (gate_column * own_rows.astype(jnp.float32)).astype(jnp.bfloat16)
    scaled_other = (other_gates * other_rows.astype(jnp.float32)).astype(jnp.bfloat16)
    grad_own = lax.dot_general(
        hidden, scaled_own, contract_rows, preferred_element_type=jnp.float32
    )
    grad_other = lax.dot_general(
        hidden_other, scaled_other, contract_rows, preferred_element_type=jnp.float32
    )
    rounded_own = lax.optimization_barrier(grad_own.astype(jnp.bfloat16))
    rounded_other = lax.optimization_barrier(grad_other.astype(jnp.bfloat16))
    partial_back, rounded_own, rounded_other = lax.optimization_barrier(
        (partial_back, rounded_own, rounded_other)
    )
    upstream = partial_own + partial_back
    down_grad = (rounded_own.astype(jnp.float32) + rounded_other.astype(jnp.float32)).astype(
        jnp.bfloat16
    )
    score = jnp.sum(hidden.astype(jnp.float32) * upstream, axis=1)
    hidden_grad = gate_column * upstream
    gate_grad = (hidden_grad * up_float * slope).astype(jnp.bfloat16)
    up_grad = (hidden_grad * active).astype(jnp.bfloat16)
    summed_scores = lax.psum(score, "tensor")
    returned = lax.all_to_all(
        summed_scores.reshape(expert_count, capacity),
        "expert",
        split_axis=0,
        concat_axis=0,
        tiled=True,
    )
    flat_scores = returned.reshape(-1)
    router_grad = jnp.stack(
        [
            jnp.sum(jnp.where(matches[which], flat_scores[None, :], 0.0), axis=1)
            for which in range(choices_each)
        ],
        axis=1,
    )
    return (gate_grad[None], up_grad[None], down_grad[None], router_grad)


def solution(mesh):
    placed = (
        P(("dp", "expert"), "tensor"),
        P(("dp", "expert"), None),
        P(("dp", "expert"), None),
        P("expert", "dp", "tensor"),
        P("expert", "dp", "tensor"),
        P("expert", "tensor", "dp"),
    )
    return jax.shard_map(
        local,
        mesh=mesh,
        in_specs=placed,
        out_specs=(
            P("expert", "dp", "tensor"),
            P("expert", "dp", "tensor"),
            P("expert", "tensor", "dp"),
            P(("dp", "expert"), None),
        ),
        check_vma=False,
    )
```

profile of v0, /device:TPU:1, one launch (start us, length us, event | category | flops | bytes accessed | tf_op | source)
XLA Modules:
  0.0 616.6 jit_solution(12437453717802722302)
XLA Ops:
  7.2 0.0 copy-start
  7.2 0.0 all-gather.3.cloned.1.call-start
  7.2 0.9 copy.28
  8.1 0.1 eq.59
  8.2 0.1 eq.55
  8.4 1.2 reduce-window.6
  9.6 0.2 slice_reduce_fusion
  9.8 0.2 reduce-window.9
  10.0 0.1 add_bitcast_fusion
  10.1 0.1 reduce_sum.48
  10.3 0.1 copy.30
  10.3 0.7 multiply_add_fusion
  11.1 8.8 %fusion.5 = bf16[768,3584]{1,0:T(8,128)(2,1)} fusion(bf16[1,768,3584]{2,1,0:T(8,128)(2,1)} %param.10, bf16[1,768,3584]{2,1,0:T(8,128)(2,1)} %param.9), kind=kLoop, calls=%fused_computation.13 | loop fusion | flops 22020096 | bytes 16515072 | tf_op jit(solution)/shard_map/convert_element_type | solution.py:44
  19.9 0.8 convolution_convert_fusion.2
  20.7 23.2 %all_to_all.20 = bf16[4,192,1024]{2,1,0:T(8,128)(2,1)} all-to-all(bf16[4,192,1024]{2,1,0:T(8,128)(2,1)S(1)} %bitcast.61), channel_id=1, replica_groups=mesh['dp'=2,'expert'=4,'tensor'=4] {'expert'}, dimensions={0} | all-to-all | bytes 3145728 | tf_op jit(solution)/shard_map/all_to_all | solution.py:53
  43.9 0.0 all-gather.3.cloned.1.call-update
  43.9 0.0 all-gather.5.cloned.1.call-start
  44.0 1.8 collective-permute-start
  45.7 115.1 %all-gather.3.cloned.1.call-done = bf16[768,4096]{1,0:T(8,128)(2,1)} async-done(((bf16[768,1024]{1,0:T(8,128)(2,1)}), bf16[768,4096]{1,0:T(8,128)(2,1)}) %all-gather.3.cloned.1.call-update) | async-done | bytes 6291472 | tf_op jit(solution)/shard_map/all_gather | solution.py:59
  160.8 1.2 constant_dynamic-slice_fusion
  162.0 1.2 collective-permute-start.1
  163.2 18.3 %collective-permute-done.1 = bf16[768,512]{1,0:T(8,128)(2,1)S(1)} collective-permute-done((bf16[768,512]{1,0:T(8,128)(2,1)S(1)}, bf16[768,512]{1,0:T(8,128)(2,1)S(1)}, u32[]{:S(2)}, u32[]{:S(2)}) %collective-permute-start.1) | collective-permute-done | bytes 786464 | tf_op jit(solution)/shard_map/ppermute | solution.py:15
  181.5 0.9 copy-done.2
  182.4 0.0 all-gather.5.cloned.1.call-update
  182.4 0.0 copy-start.3
  182.5 0.0 collective-permute-done
  182.5 64.6 %all-gather.5.cloned.1.call-done = bf16[768,2048]{1,0:T(8,128)(2,1)} async-done(((bf16[768,512]{1,0:T(8,128)(2,1)}), bf16[768,2048]{1,0:T(8,128)(2,1)}) %all-gather.5.cloned.1.call-update) | async-done | bytes 3145744 | tf_op jit(solution)/shard_map/all_gather | solution.py:68
  247.0 18.2 %fusion.1 = f32[768,3584]{1,0:T(8,128)} fusion(bf16[768,2048]{1,0:T(8,128)(2,1)} %all-gather.5.cloned.1.call-done, bf16[1,3584,2048]{2,1,0:T(8,128)(2,1)} %param.11), kind=kOutput, calls=%fused_computation.7 | convolution fusion | flops 11274289152 | bytes 28835840 | tf_op jit(solution)/shard_map/dot_general | solution.py:72
  265.2 1.2 collective-permute-start.2
  266.4 0.2 select_reduce_fusion.2
  266.6 0.1 convert_element_type.113
  266.7 7.0 %all_to_all.21 = bf16[4,1,192]{2,1,0:T(2,128)(2,1)S(1)} all-to-all(bf16[4,1,192]{2,1,0:T(2,128)(2,1)S(1)} %convert_element_type.113), channel_id=1, replica_groups=mesh['dp'=2,'expert'=4,'tensor'=4] {'expert'}, dimensions={0} | all-to-all | bytes 3072 | tf_op jit(solution)/shard_map/all_to_all | solution.py:54
  273.7 0.1 reshape.71
  273.8 0.3 collective-permute-start.3
  274.1 229.0 %collective-permute-done.3 = bf16[768]{0:T(1024)(128)(2,1)S(1)} collective-permute-done((bf16[768]{0:T(1024)(128)(2,1)S(1)}, bf16[768]{0:T(1024)(128)(2,1)S(1)}, u32[]{:S(2)}, u32[]{:S(2)}) %collective-permute-start.3) | collective-permute-done | bytes 1568 | tf_op jit(solution)/shard_map/ppermute | solution.py:15
  503.1 18.3 %convolution_convert_fusion.1 = bf16[3584,2048]{1,0:T(8,128)(2,1)} fusion(bf16[768,3584]{1,0:T(8,128)(2,1)} %fusion.5, f32[768]{0:T(1024)S(1)} %convert_element_type.91, bf16[768,4096]{1,0:T(8,128)(2,1)} %all-gather.3.cloned.1.call-done, s32[]{:T(128)S(6)} %select_n.31), kind=kOutput, calls=%fused_computation.5 | convolution fusion | flops 11286347776 | bytes 23333892 | tf_op jit(solution)/shard_map/dot_general | solution.py:81
  521.3 18.3 %fusion.3 = f32[768,3584]{1,0:T(8,128)} fusion(bf16[1,3584,2048]{2,1,0:T(8,128)(2,1)} %param.11, bf16[768,4096]{1,0:T(8,128)(2,1)} %all-gather.3.cloned.1.call-done, s32[]{:T(128)S(6)} %select_n.31), kind=kOutput, calls=%fused_computation.9 | convolution fusion | flops 11274289152 | bytes 28835844 | tf_op jit(solution)/shard_map/dot_general | solution.py:76
  539.6 17.9 %convolution_convert_fusion = bf16[3584,2048]{1,0:T(8,128)(2,1)} fusion(bf16[768,3584]{1,0:T(8,128)(2,1)} %collective-permute-done, bf16[768,2048]{1,0:T(8,128)(2,1)} %all-gather.5.cloned.1.call-done, f32[768]{0:T(1024)S(1)} %convert_element_type.101), kind=kOutput, calls=%fused_computation.4 | convolution fusion | flops 11286347776 | bytes 23333888 | tf_op jit(solution)/shard_map/dot_general | solution.py:84
  557.5 0.0 collective-permute-done.2
  557.5 17.8 %fusion.13 = (bf16[1,768,3584]{2,1,0:T(8,128)(2,1)}, bf16[1,768,3584]{2,1,0:T(8,128)(2,1)}, f32[768]{0:T(1024)S(1)}) fusion(f32[768]{0:T(1024)S(1)} %convert_element_type.91, bf16[1,768,3584]{2,1,0:T(8,128)(2,1)S(1)} %bitcast.59, f32[768,3584]{1,0:T(8,128)} %fusion.3, f32[768,3584]{1,0:T(8,128)} %collective-permute-done.2, bf16[1,768,3584]{2,1,0:T(8,128)(2,1)} %param.10, ...), kind=kLoop, calls=%fused_computation.25 | loop fusion | flops 55049472 | bytes 49551360 | tf_op jit(solution)/shard_map/broadcast_in_dim | solution.py:116
  575.4 0.1 all_to_all.15
  575.4 8.4 %psum.7 = f32[4,1,192]{2,1,0:T(1,128)} all-reduce(f32[4,1,192]{2,1,0:T(1,128)S(1)} %all_to_all.15), channel_id=1, replica_groups=mesh['dp'=2,'expert'=4,'tensor'=4] {'tensor'}, use_global_device_ids=true, to_apply=%region_5.6 | all-reduce | flops 768 | bytes 6144 | tf_op jit(solution)/shard_map/psum | solution.py:100
  583.9 6.2 %all-to-all-start.2 = ((f32[4,1,192]{2,1,0:T(1,128)}), f32[4,1,192]{2,1,0:T(1,128)S(1)}, u32[]{:S(2)}, u32[]{:S(2)}) async-start(f32[4,1,192]{2,1,0:T(1,128)} %psum.7), calls=%async_computation.2 | async-start | bytes 8192 | tf_op jit(solution)/shard_map/all_to_all | solution.py:101
  590.1 18.7 %fusion = bf16[1,3584,2048]{2,1,0:T(8,128)(2,1)} fusion(bf16[3584,2048]{1,0:T(8,128)(2,1)} %convolution_convert_fusion, bf16[3584,2048]{1,0:T(8,128)(2,1)} %convolution_convert_fusion.1), kind=kLoop, calls=%fused_computation.6 | loop fusion | flops 29360128 | bytes 44040192 | tf_op jit(solution)/shard_map/broadcast_in_dim | solution.py:116
  608.7 0.0 all-to-all-done.2
  608.8 0.1 broadcast_in_dim.76
  608.8 0.3 select_reduce_fusion.1
  609.2 0.6 pad_maximum_fusion
  (18 shorter events, 0.1 us)
Async XLA Ops:
  7.2 12.7 %copy-start = (bf16[256,1024]{1,0:T(8,128)(2,1)S(1)}, bf16[256,1024]{1,0:T(8,128)(2,1)}, u32[]{:S(2)}) copy-start(bf16[256,1024]{1,0:T(8,128)(2,1)} %param.6) | copy-start | bytes 1572868
  7.2 153.6 %all-gather.3.cloned.1.call-start = ((), (), s32[]{:S(2)}) async-start(), calls=%async_computation.3 | async-start | bytes 7864320 | tf_op jit(solution)/shard_map/all_gather | solution.py:59
  43.9 203.1 %all-gather.5.cloned.1.call-start = ((), (), s32[]{:S(2)}) async-start(), calls=%async_computation.4 | async-start | bytes 3932160 | tf_op jit(solution)/shard_map/all_gather | solution.py:68
  44.0 138.5 %collective-permute-start = (bf16[768,3584]{1,0:T(8,128)(2,1)}, bf16[768,3584]{1,0:T(8,128)(2,1)}, u32[]{:S(2)}, u32[]{:S(2)}) collective-permute-start(bf16[768,3584]{1,0:T(8,128)(2,1)} %fusion.5), channel_id=1, source_target_pairs={{0,16},{16,0},{1,17},{17,1},{2,18},{18,2},{3,19},{19,3},{4,20},{20... | collective-permute-start | bytes 16515080 | tf_op jit(solution)/shard_map/ppermute | solution.py:15
  162.0 19.6 %collective-permute-start.1 = (bf16[768,512]{1,0:T(8,128)(2,1)S(1)}, bf16[768,512]{1,0:T(8,128)(2,1)S(1)}, u32[]{:S(2)}, u32[]{:S(2)}) collective-permute-start(bf16[768,512]{1,0:T(8,128)(2,1)S(1)} %constant_dynamic-slice_fusion), channel_id=1, source_target_pairs={{0,16},{16,0},{1,17},{17,1},{2,18},{18,2},{3,19},{19,3},{4,20},{20... | collective-permute-start | bytes 2359304 | tf_op jit(solution)/shard_map/ppermute | solution.py:15
  181.5 0.9 copy-start.2
  182.4 83.9 %copy-start.3 = (bf16[256,2]{0,1:T(2,128)(2,1)S(1)}, bf16[256,2]{0,1:T(2,128)(2,1)}, u32[]{:S(2)}) copy-start(bf16[256,2]{0,1:T(2,128)(2,1)} %param.8) | copy-start | bytes 3076
  265.2 292.3 %collective-permute-start.2 = (f32[768,3584]{1,0:T(8,128)}, f32[768,3584]{1,0:T(8,128)}, u32[]{:S(2)}, u32[]{:S(2)}) collective-permute-start(f32[768,3584]{1,0:T(8,128)} %fusion.1), channel_id=1, source_target_pairs={{0,16},{16,0},{1,17},{17,1},{2,18},{18,2},{3,19},{19,3},{4,20},{20... | collective-permute-start | bytes 33030152 | tf_op jit(solution)/shard_map/ppermute | solution.py:15
  273.8 229.3 %collective-permute-start.3 = (bf16[768]{0:T(1024)(128)(2,1)S(1)}, bf16[768]{0:T(1024)(128)(2,1)S(1)}, u32[]{:S(2)}, u32[]{:S(2)}) collective-permute-start(bf16[768]{0:T(1024)(128)(2,1)S(1)} %reshape.71), channel_id=1, source_target_pairs={{0,16},{16,0},{1,17},{17,1},{2,18},{18,2},{3,19},{19,3},{4,20},{20... | collective-permute-start | bytes 4616 | tf_op jit(solution)/shard_map/ppermute | solution.py:15
  503.1 54.5 %slice-start = ((s8[5505024]{0:T(1024)(128)(4,1)}), s8[4194304]{0:T(1024)(128)(4,1)S(1)}, s32[]{:S(2)}) async-start(s8[5505024]{0:T(1024)(128)(4,1)} %bitcast.58), calls=%async_computation.5 | async-start | bytes 8388608
  521.3 36.2 %slice-start.1 = ((s8[5505024]{0:T(1024)(128)(4,1)}), s8[1310720]{0:T(1024)(128)(4,1)S(1)}, s32[]{:S(2)}) async-start(s8[5505024]{0:T(1024)(128)(4,1)} %bitcast.58), calls=%async_computation.6 | async-start | bytes 2621440
  583.9 24.9 %all-to-all-start.2 = ((f32[4,1,192]{2,1,0:T(1,128)}), f32[4,1,192]{2,1,0:T(1,128)S(1)}, u32[]{:S(2)}, u32[]{:S(2)}) async-start(f32[4,1,192]{2,1,0:T(1,128)} %psum.7), calls=%async_computation.2 | async-start | bytes 8192 | tf_op jit(solution)/shard_map/all_to_all | solution.py:101
  590.1 19.7 %copy-start.1 = (bf16[256,1024]{1,0:T(8,128)(2,1)S(1)}, bf16[256,1024]{1,0:T(8,128)(2,1)}, u32[]{:S(2)}) copy-start(bf16[256,1024]{1,0:T(8,128)(2,1)} %param.6) | copy-start | bytes 1572868
Sparse Core Ops, SparseCore 0:
  44.1 116.7 all-gather.2
  182.6 64.4 all-gather.4
where the time goes:
time: 617 us
  waiting for transfers between devices  427 us (69%)
  matrix products  73.4 us (12%)
  other arithmetic  48.8 us (8%)
  blocking collectives  38.6 us (6%)
  between operations  14.1 us (2%)
  starting transfers between devices  10.7 us (2%)
    ppermute x4, waiting for transfers between devices, swap_dp(): return lax.ppermute(value, 'dp', perm=[(0, 1), (1, 0)])  247 us
    all_gather x1, waiting for transfers between devices, local(): fragment = lax.all_gather(narrow_rows, 'tensor', axis=1, tiled=True)  115 us
    all_gather x1, waiting for transfers between devices, local(): other_rows = lax.all_gather(other_piece, 'tensor', axis=1, tiled=True)  64.6 us
    broadcast_in_dim x2, other arithmetic, local(): return (gate_grad[None], up_grad[None], down_grad[None], router_grad)  36.5 us
    all_to_all x1, blocking collectives, local(): lax.all_to_all(outgoing, 'expert', split_axis=0, concat_axis=0, tiled=True)  23.2 us
    dot_general x1, matrix products, local(): lax.dot_general(own_rows, local_weight, contract_cols, preferred_element_...  18.3 us
    dot_general x1, matrix products, local(): lax.dot_general(hidden, scaled_own, contract_rows, preferred_element_type...  18.3 us
    dot_general x1, matrix products, local(): lax.dot_general(other_rows, local_weight, contract_cols, preferred_elemen...  18.2 us
  transfers between devices with their start and end apart: 7, of which 4 were waited for; matrix products, arithmetic and copies ran while one was open for 12% of the time, Pallas kernels for 0%

commit v1 on v0

--- a/solution.py
+++ b/solution.py
@@ -50,7 +50,18 @@
     outgoing = outgoing.astype(jnp.bfloat16).reshape(expert_count, capacity, -1)
     hidden, outgoing = lax.optimization_barrier((hidden, outgoing))
     hidden_other = swap_dp(hidden)
-    received = lax.all_to_all(outgoing, "expert", split_axis=0, concat_axis=0, tiled=True)
+    ways, here = (lax.axis_size("expert"), lax.axis_index("expert"))
+    width_2 = outgoing.shape[0] // ways
+    shape = list(outgoing.shape)
+    shape[0] = width_2
+    height = shape[0]
+    shape[0] = height * ways
+    received = jnp.zeros(shape, outgoing.dtype)
+    for mask in range(ways):
+        part_2 = lax.dynamic_slice_in_dim(outgoing, (here ^ mask) * width_2, width_2, axis=0)
+        if mask:
+            part_2 = lax.ppermute(part_2, "expert", [(d, d ^ mask) for d in range(ways)])
+        received = lax.dynamic_update_slice_in_dim(received, part_2, (here ^ mask) * height, axis=0)
     gate_slots = lax.all_to_all(gate_send, "expert", split_axis=0, concat_axis=0, tiled=True)
     slots = expert_count * capacity
     narrow_rows = received.reshape(slots, -1)

time: 617 us -> 607 us (0.984)
  blocking collectives: 38.6 us -> 15.4 us
  waiting for transfers between devices: 427 us -> 445 us
  other arithmetic: 48.8 us -> 30.9 us
  matrix products: 73.4 us -> 80.1 us
    all_to_all x1 -> x0, blocking collectives: 23.2 us -> none  [local(): lax.all_to_all(outgoing, 'expert', split_axis=0, concat_axis=0, tiled=True)]
    broadcast_in_dim x2 -> x1, other arithmetic: 36.5 us -> 18.7 us  [local(): return (gate_grad[None], up_grad[None], down_grad[None], router_grad)]
    ppermute x0 -> x3, waiting for transfers between devices: none -> 17.7 us  [local(): lax.ppermute(part_2, 'expert', [(d, d ^ mask) for d in range(ways)])]
    dot_general x1, matrix products: 18.3 us -> 24.8 us  [local(): lax.dot_general(own_rows, local_weight, contract_cols, preferred_element_...]
  transfers between devices with their start and end apart: 7 -> 10, of which waited for: 4 -> 6; matrix products, arithmetic and copies ran while one was open for 12% -> 9% of each run, Pallas kernels for 0% -> 0%
where the time goes in v1:
time: 607 us; the launch traced here: 606 us
  waiting for transfers between devices  445 us (73%)
  matrix products  80.1 us (13%)
  other arithmetic  30.9 us (5%)
  blocking collectives  15.4 us (3%)
  between operations  14.2 us (2%)
  starting transfers between devices  13.3 us (2%)
  local copies, waits for them, and re-layouts  6.91 us (1%)
    ppermute x4, waiting for transfers between devices, swap_dp(): return lax.ppermute(value, 'dp', perm=[(0, 1), (1, 0)])  247 us
    all_gather x1, waiting for transfers between devices, local(): fragment = lax.all_gather(narrow_rows, 'tensor', axis=1, tiled=True)  115 us
    all_gather x1, waiting for transfers between devices, local(): other_rows = lax.all_gather(other_piece, 'tensor', axis=1, tiled=True)  65.4 us
    dot_general x1, matrix products, local(): lax.dot_general(own_rows, local_weight, contract_cols, preferred_element_...  24.8 us
    broadcast_in_dim x1, other arithmetic, local(): return (gate_grad[None], up_grad[None], down_grad[None], router_grad)  18.7 us
    dot_general x1, matrix products, local(): lax.dot_general(hidden, scaled_own, contract_rows, preferred_element_type...  18.3 us
    dot_general x1, matrix products, local(): lax.dot_general(other_rows, local_weight, contract_cols, preferred_elemen...  18.2 us
    ppermute x3, waiting for transfers between devices, local(): lax.ppermute(part_2, 'expert', [(d, d ^ mask) for d in range(ways)])  17.7 us
  transfers between devices with their start and end apart: 10, of which 6 were waited for; matrix products, arithmetic and copies ran while one was open for 9% of the time, Pallas kernels for 0%

profile of v1, /device:TPU:1, one launch (start us, length us, event | category | flops | bytes accessed | tf_op | source)
XLA Modules:
  0.0 606.2 jit_solution(898286910435385008)
XLA Ops:
  7.2 0.0 all-gather.3.cloned.1.call-start
  7.2 0.9 copy.28
  8.1 0.1 eq.59
  8.3 0.1 eq.55
  8.4 1.2 reduce-window.6
  9.6 0.2 slice_reduce_fusion
  9.9 0.2 reduce-window.9
  10.0 0.1 add_bitcast_fusion
  10.1 0.1 reduce_sum.48
  10.3 0.1 copy.30
  10.4 0.7 multiply_add_fusion
  11.1 8.8 %fusion.5 = bf16[768,3584]{1,0:T(8,128)(2,1)} fusion(bf16[1,768,3584]{2,1,0:T(8,128)(2,1)} %param.10, bf16[1,768,3584]{2,1,0:T(8,128)(2,1)} %param.9), kind=kLoop, calls=%fused_computation.13 | loop fusion | flops 22020096 | bytes 16515072 | tf_op jit(solution)/shard_map/convert_element_type | solution.py:44
  19.9 1.9 convolution_convert_fusion.2
  21.8 0.2 broadcast_in_dim.74
  22.0 1.5 constant_dynamic-slice_fusion.1
  23.5 0.1 collective-permute-start
  23.6 2.7 collective-permute-start.1
  26.3 0.0 collective-permute-start.2
  26.4 9.3 %collective-permute-done.1 = bf16[1,192,1024]{2,1,0:T(8,128)(2,1)S(1)} collective-permute-done((bf16[1,192,1024]{2,1,0:T(8,128)(2,1)S(1)}, bf16[1,192,1024]{2,1,0:T(8,128)(2,1)S(1)}, u32[]{:S(2)}, u32[]{:S(2)}) %collective-permute-start.1) | collective-permute-done | bytes 393248 | tf_op jit(solution)/shard_map/ppermute | solution.py:63
  35.8 8.4 %collective-permute-done.2 = bf16[1,192,1024]{2,1,0:T(8,128)(2,1)S(1)} collective-permute-done((bf16[1,192,1024]{2,1,0:T(8,128)(2,1)S(1)}, bf16[1,192,1024]{2,1,0:T(8,128)(2,1)S(1)}, u32[]{:S(2)}, u32[]{:S(2)}) %collective-permute-start.2) | collective-permute-done | bytes 393248 | tf_op jit(solution)/shard_map/ppermute | solution.py:63
  44.2 1.1 copy-done.2
  45.3 0.0 all-gather.3.cloned.1.call-update
  45.4 0.0 all-gather.5.cloned.1.call-start
  45.4 1.5 collective-permute-start.3
  46.9 115.2 %all-gather.3.cloned.1.call-done = bf16[768,4096]{1,0:T(8,128)(2,1)} async-done(((bf16[768,1024]{1,0:T(8,128)(2,1)}), bf16[768,4096]{1,0:T(8,128)(2,1)}) %all-gather.3.cloned.1.call-update) | async-done | bytes 6291472 | tf_op jit(solution)/shard_map/all_gather | solution.py:70
  162.1 1.2 constant_dynamic-slice_fusion
  163.3 1.2 collective-permute-start.4
  164.6 18.1 %collective-permute-done.4 = bf16[768,512]{1,0:T(8,128)(2,1)S(1)} collective-permute-done((bf16[768,512]{1,0:T(8,128)(2,1)S(1)}, bf16[768,512]{1,0:T(8,128)(2,1)S(1)}, u32[]{:S(2)}, u32[]{:S(2)}) %collective-permute-start.4) | collective-permute-done | bytes 786464 | tf_op jit(solution)/shard_map/ppermute | solution.py:15
  182.6 0.9 copy-done.3
  183.6 65.4 %all-gather.5.cloned.1.call-done = bf16[768,2048]{1,0:T(8,128)(2,1)} async-done(((bf16[768,512]{1,0:T(8,128)(2,1)}), bf16[768,2048]{1,0:T(8,128)(2,1)}) %all-gather.5.cloned.1.call-update) | async-done | bytes 3145744 | tf_op jit(solution)/shard_map/all_gather | solution.py:79
  248.9 18.2 %fusion.1 = f32[768,3584]{1,0:T(8,128)} fusion(bf16[768,2048]{1,0:T(8,128)(2,1)} %all-gather.5.cloned.1.call-done, bf16[1,3584,2048]{2,1,0:T(8,128)(2,1)} %param.11), kind=kOutput, calls=%fused_computation.7 | convolution fusion | flops 11274289152 | bytes 28835840 | tf_op jit(solution)/shard_map/dot_general | solution.py:83
  267.1 1.2 collective-permute-start.5
  268.3 0.2 select_reduce_fusion.2
  268.6 0.1 convert_element_type.113
  268.6 7.0 %all_to_all.15 = bf16[4,1,192]{2,1,0:T(2,128)(2,1)S(1)} all-to-all(bf16[4,1,192]{2,1,0:T(2,128)(2,1)S(1)} %convert_element_type.113), channel_id=1, replica_groups=mesh['dp'=2,'expert'=4,'tensor'=4] {'expert'}, dimensions={0} | all-to-all | bytes 3072 | tf_op jit(solution)/shard_map/all_to_all | solution.py:65
  275.7 0.1 reshape.71
  275.7 0.3 collective-permute-start.6
  276.0 229.0 %collective-permute-done.6 = bf16[768]{0:T(1024)(128)(2,1)S(1)} collective-permute-done((bf16[768]{0:T(1024)(128)(2,1)S(1)}, bf16[768]{0:T(1024)(128)(2,1)S(1)}, u32[]{:S(2)}, u32[]{:S(2)}) %collective-permute-start.6) | collective-permute-done | bytes 1568 | tf_op jit(solution)/shard_map/ppermute | solution.py:15
  505.0 18.3 %convolution_convert_fusion.1 = bf16[3584,2048]{1,0:T(8,128)(2,1)} fusion(bf16[768,3584]{1,0:T(8,128)(2,1)} %fusion.5, f32[768]{0:T(1024)S(1)} %convert_element_type.91, bf16[768,4096]{1,0:T(8,128)(2,1)} %all-gather.3.cloned.1.call-done, s32[]{:T(128)S(6)} %select_n.51), kind=kOutput, calls=%fused_computation.5 | convolution fusion | flops 11286347776 | bytes 23333892 | tf_op jit(solution)/shard_map/dot_general | solution.py:92
  523.3 16.9 %convolution_convert_fusion = bf16[3584,2048]{1,0:T(8,128)(2,1)} fusion(bf16[768,3584]{1,0:T(8,128)(2,1)} %collective-permute-done.3, bf16[768,2048]{1,0:T(8,128)(2,1)S(1)} %copy-done.5, f32[768]{0:T(1024)S(1)} %convert_element_type.101), kind=kOutput, calls=%fused_computation.4 | convolution fusion | flops 11286347776 | bytes 23333888 | tf_op jit(solution)/shard_map/dot_general | solution.py:95
  540.2 24.8 %fusion.16 = (bf16[1,768,3584]{2,1,0:T(8,128)(2,1)}, bf16[1,768,3584]{2,1,0:T(8,128)(2,1)}, f32[768]{0:T(1024)S(1)}) fusion(f32[768]{0:T(1024)S(1)} %convert_element_type.91, bf16[1,768,3584]{2,1,0:T(8,128)(2,1)} %param.9, bf16[1,768,3584]{2,1,0:T(8,128)(2,1)} %param.10, bf16[768,3584]{1,0:T(8,128)(2,1)} %fusion.5, f32[768,3584]{1,0:T(8,128)} %collective-permute-done.5, ...), kind=kOutput, calls=%fused_computation.26 | convolution fusion | flops 11329338368 | bytes 56367108 | tf_op jit(solution)/shard_map/dot_general | solution.py:87
  565.0 0.1 all_to_all.11
  565.1 8.4 %psum.7 = f32[4,1,192]{2,1,0:T(1,128)} all-reduce(f32[4,1,192]{2,1,0:T(1,128)S(1)} %all_to_all.11), channel_id=1, replica_groups=mesh['dp'=2,'expert'=4,'tensor'=4] {'tensor'}, use_global_device_ids=true, to_apply=%region_5.6 | all-reduce | flops 768 | bytes 6144 | tf_op jit(solution)/shard_map/psum | solution.py:111
  573.5 6.2 %all-to-all-start.1 = ((f32[4,1,192]{2,1,0:T(1,128)}), f32[4,1,192]{2,1,0:T(1,128)S(1)}, u32[]{:S(2)}, u32[]{:S(2)}) async-start(f32[4,1,192]{2,1,0:T(1,128)} %psum.7), calls=%async_computation.1 | async-start | bytes 8192 | tf_op jit(solution)/shard_map/all_to_all | solution.py:112
  579.7 18.7 %fusion = bf16[1,3584,2048]{2,1,0:T(8,128)(2,1)} fusion(bf16[3584,2048]{1,0:T(8,128)(2,1)} %convolution_convert_fusion, bf16[3584,2048]{1,0:T(8,128)(2,1)} %convolution_convert_fusion.1), kind=kLoop, calls=%fused_computation.6 | loop fusion | flops 29360128 | bytes 44040192 | tf_op jit(solution)/shard_map/broadcast_in_dim | solution.py:127
  598.4 0.1 broadcast_in_dim.80
  598.5 0.3 select_reduce_fusion.1
  598.8 0.6 pad_maximum_fusion
  (26 shorter events, 0.2 us)
Async XLA Ops:
  7.2 12.8 %copy-start = (bf16[256,1024]{1,0:T(8,128)(2,1)S(1)}, bf16[256,1024]{1,0:T(8,128)(2,1)}, u32[]{:S(2)}) copy-start(bf16[256,1024]{1,0:T(8,128)(2,1)} %param.6) | copy-start | bytes 1572868
  7.2 154.9 %all-gather.3.cloned.1.call-start = ((), (), s32[]{:S(2)}) async-start(), calls=%async_computation.2 | async-start | bytes 7864320 | tf_op jit(solution)/shard_map/all_gather | solution.py:70
  23.5 2.9 collective-permute-start
  23.6 12.1 %collective-permute-start.1 = (bf16[1,192,1024]{2,1,0:T(8,128)(2,1)S(1)}, bf16[1,192,1024]{2,1,0:T(8,128)(2,1)S(1)}, u32[]{:S(2)}, u32[]{:S(2)}) collective-permute-start(bf16[1,192,1024]{2,1,0:T(8,128)(2,1)S(1)} %get-tuple-element.24), channel_id=1, source_target_pairs={{0,8},{4,12},{8,0},{12,4},{1,9},{5,13},{9,1},{13,5},{2,10},{6,14},... | collective-permute-start | bytes 1179656 | tf_op jit(solution)/shard_map/ppermute | solution.py:63
  26.3 17.8 %collective-permute-start.2 = (bf16[1,192,1024]{2,1,0:T(8,128)(2,1)S(1)}, bf16[1,192,1024]{2,1,0:T(8,128)(2,1)S(1)}, u32[]{:S(2)}, u32[]{:S(2)}) collective-permute-start(bf16[1,192,1024]{2,1,0:T(8,128)(2,1)S(1)} %get-tuple-element.23), channel_id=1, source_target_pairs={{0,12},{4,8},{8,4},{12,0},{1,13},{5,9},{9,5},{13,1},{2,14},{6,10},... | collective-permute-start | bytes 1179656 | tf_op jit(solution)/shard_map/ppermute | solution.py:63
  44.2 1.1 copy-start.2
  45.4 203.6 %all-gather.5.cloned.1.call-start = ((), (), s32[]{:S(2)}) async-start(), calls=%async_computation.3 | async-start | bytes 3932160 | tf_op jit(solution)/shard_map/all_gather | solution.py:79
  45.4 138.1 %collective-permute-start.3 = (bf16[768,3584]{1,0:T(8,128)(2,1)}, bf16[768,3584]{1,0:T(8,128)(2,1)}, u32[]{:S(2)}, u32[]{:S(2)}) collective-permute-start(bf16[768,3584]{1,0:T(8,128)(2,1)} %fusion.5), channel_id=1, source_target_pairs={{0,16},{16,0},{1,17},{17,1},{2,18},{18,2},{3,19},{19,3},{4,20},{20... | collective-permute-start | bytes 16515080 | tf_op jit(solution)/shard_map/ppermute | solution.py:15
  163.3 19.3 %collective-permute-start.4 = (bf16[768,512]{1,0:T(8,128)(2,1)S(1)}, bf16[768,512]{1,0:T(8,128)(2,1)S(1)}, u32[]{:S(2)}, u32[]{:S(2)}) collective-permute-start(bf16[768,512]{1,0:T(8,128)(2,1)S(1)} %constant_dynamic-slice_fusion), channel_id=1, source_target_pairs={{0,16},{16,0},{1,17},{17,1},{2,18},{18,2},{3,19},{19,3},{4,20},{20... | collective-permute-start | bytes 2359304 | tf_op jit(solution)/shard_map/ppermute | solution.py:15
  182.6 0.9 copy-start.3
  183.5 84.8 %copy-start.4 = (bf16[256,2]{0,1:T(2,128)(2,1)S(1)}, bf16[256,2]{0,1:T(2,128)(2,1)}, u32[]{:S(2)}) copy-start(bf16[256,2]{0,1:T(2,128)(2,1)} %param.8) | copy-start | bytes 3076
  267.1 273.0 %collective-permute-start.5 = (f32[768,3584]{1,0:T(8,128)}, f32[768,3584]{1,0:T(8,128)}, u32[]{:S(2)}, u32[]{:S(2)}) collective-permute-start(f32[768,3584]{1,0:T(8,128)} %fusion.1), channel_id=1, source_target_pairs={{0,16},{16,0},{1,17},{17,1},{2,18},{18,2},{3,19},{19,3},{4,20},{20... | collective-permute-start | bytes 33030152 | tf_op jit(solution)/shard_map/ppermute | solution.py:15
  275.7 229.3 %collective-permute-start.6 = (bf16[768]{0:T(1024)(128)(2,1)S(1)}, bf16[768]{0:T(1024)(128)(2,1)S(1)}, u32[]{:S(2)}, u32[]{:S(2)}) collective-permute-start(bf16[768]{0:T(1024)(128)(2,1)S(1)} %reshape.71), channel_id=1, source_target_pairs={{0,16},{16,0},{1,17},{17,1},{2,18},{18,2},{3,19},{19,3},{4,20},{20... | collective-permute-start | bytes 4616 | tf_op jit(solution)/shard_map/ppermute | solution.py:15
  505.0 18.3 %copy-start.5 = (bf16[768,2048]{1,0:T(8,128)(2,1)S(1)}, bf16[768,2048]{1,0:T(8,128)(2,1)}, u32[]{:S(2)}) copy-start(bf16[768,2048]{1,0:T(8,128)(2,1)} %all-gather.5.cloned.1.call-done) | copy-start | bytes 9437188
  573.5 24.9 %all-to-all-start.1 = ((f32[4,1,192]{2,1,0:T(1,128)}), f32[4,1,192]{2,1,0:T(1,128)S(1)}, u32[]{:S(2)}, u32[]{:S(2)}) async-start(f32[4,1,192]{2,1,0:T(1,128)} %psum.7), calls=%async_computation.1 | async-start | bytes 8192 | tf_op jit(solution)/shard_map/all_to_all | solution.py:112
  579.7 19.7 %copy-start.1 = (bf16[256,1024]{1,0:T(8,128)(2,1)S(1)}, bf16[256,1024]{1,0:T(8,128)(2,1)}, u32[]{:S(2)}) copy-start(bf16[256,1024]{1,0:T(8,128)(2,1)} %param.6) | copy-start | bytes 1572868
Sparse Core Ops, SparseCore 0:
  45.5 116.5 all-gather.2
  183.7 65.2 all-gather.4
